TPU v7x, 32 devices: a whole 2x2x4 slice. The times are simulated.
32 devices in a mesh: dp: 16 (over z, y, core), head: 2 (over x).
Axes of the slice: x: 2, y: 2, z: 4, core: 2. Of those that a mesh axis runs over, the one named last changes fastest.
Arguments:
- layer_input: bfloat16 [16, 256, 768], P('dp', 'head'), may hold values from -6 to 6
- pair_input: bfloat16 [16, 256, 256, 256], P('dp', 'head'), may hold values from -6 to 6
- time_cond: float32 [16, 256], P('dp'), may hold values from -6 to 6
- chain_lengths: int32 [16], P('dp'), may hold values from 128 to 256, as said below
- residue_mask: int32 [16, 256], P('dp'), may hold values from 0 to 1, as said below
- mod_weight: bfloat16 [256, 4608], replicated, may hold values from -0.375 to 0.375
- mod_bias: float32 [4608], replicated, may hold values from -3 to 3
- qkv_weight: bfloat16 [768, 3, 768], P(None, None, 'head'), may hold values from -0.21875 to 0.21875
- pair_gain: float32 [256], replicated, may hold values from 0.25 to 1.75
- pair_weight: bfloat16 [256, 12], replicated, may hold values from -0.375 to 0.375
- out_weight: bfloat16 [768, 768], P('head'), may hold values from -0.625 to 0.625
- out_bias: float32 [768], replicated, may hold values from -3 to 3
- gate_up_weight: bfloat16 [768, 2, 3072], P(None, None, 'head'), may hold values from -0.21875 to 0.21875
- down_weight: bfloat16 [3072, 768], P('head'), may hold values from -0.21875 to 0.21875
- output_grad: bfloat16 [16, 256, 768], P('dp', 'head'), may hold values from -6 to 6
Outputs:
- layer_output: bfloat16 [16, 256, 768], P('dp', 'head')
- input_grad: float32 [16, 256, 768], P('dp', 'head')
- pair_grad: bfloat16 [16, 256, 256, 256], P('dp', 'head')
- cond_grad: float32 [16, 256], P('dp')
- mod_weight_grad: float32 [256, 4608], replicated
- mod_bias_grad: float32 [4608], replicated
- qkv_weight_grad: float32 [768, 3, 768], P('dp', None, 'head')
- pair_gain_grad: float32 [256], replicated
- pair_weight_grad: float32 [256, 12], replicated
- out_weight_grad: float32 [768, 768], P('head', 'dp')
- out_bias_grad: float32 [768], replicated
- gate_up_grad: float32 [768, 2, 3072], P('dp', None, 'head')
- down_grad: float32 [3072, 768], P('head', 'dp')
Inputs may be any that keep to these rules, and one draw needn't show every extreme that they name: `chain_lengths`: each chain has 128 to 256 residues in use; the first chain has all 256. `residue_mask`: the first residue of every chain is resolved.
All inputs are finite; a program needn't handle non-finite values.
Results may differ from a plain program's by a relative error of at most 0.014.
The roundings to bfloat16 on the way count: a program that leaves them out, or rounds other values in their place, can miss the bound.
Values may be sent and summed in bfloat16 or wider, within the bound.
No kernel may reach another device: no remote copies, remote signals or barrier semaphores. Data moves between devices by JAX's collectives and lax.ppermute only.
A program may use at most 256 MiB of HBM per device.

v0:
```python
import jax
import jax.numpy as jnp
from jax import lax
from jax.sharding import PartitionSpec as P

DH = 64
epsilon = 1e-05
masked_score = -1000000000.0
precise = lax.Precision.HIGHEST
LANES = 128


def layer_norm(values):
    centred = values - jnp.mean(values, axis=-1, keepdims=True)
    inv_std = lax.rsqrt(jnp.mean(centred * centred, axis=-1, keepdims=True) + epsilon)
    return (centred * inv_std, inv_std)


def norm_back(normed, inv_std, grad):
    mean_grad = jnp.mean(grad, axis=-1, keepdims=True)
    mean_proj = jnp.mean(grad * normed, axis=-1, keepdims=True)
    return inv_std * (grad - mean_grad - normed * mean_proj)


def silu_slope(values):
    sigma = jax.nn.sigmoid(values)
    return sigma * (1.0 + values * (1.0 - sigma))


def head_split(values):
    return values.reshape(values.shape[:-1] + (values.shape[-1] // DH, DH))


def swap_heads(values):
    return lax.ppermute(values, "head", [(0, 1), (1, 0)])


def whole_rows(own, first):
    other = swap_heads(own)
    return jnp.where(
        first, jnp.concatenate([own, other], axis=1), jnp.concatenate([other, own], axis=1)
    )


def own_rows(values, head, rows):
    return lax.dynamic_slice_in_dim(values, head * rows, rows, 1)


def head_sum(part):
    return part + swap_heads(part)


def attn_scores(queries, keys, biases, valid):
    scores = jnp.einsum("cqhe,ckhe->chqk", queries, keys, preferred_element_type=jnp.float32)
    scores = scores * DH ** (-0.5) + biases.astype(jnp.float32)
    return jnp.where(valid[:, None, None, :], scores, masked_score)


def to_chunks(values, parts):
    return values.reshape(parts, -1, LANES)


def shards(
    layer_input,
    pair_input,
    time_cond,
    chain_lengths,
    residue_mask,
    mod_weight,
    mod_bias,
    qkv_weight,
    pair_gain,
    pair_weight,
    out_weight,
    out_bias,
    gate_up_weight,
    down_weight,
    output_grad,
):
    chains = layer_input.shape[0]
    rows = layer_input.shape[1]
    width = layer_input.shape[2]
    length = residue_mask.shape[1]
    head = lax.axis_index("head")
    first = head == 0
    data_count = lax.axis_size("dp")
    x_rows = whole_rows(layer_input, first)
    g_rows = whole_rows(output_grad, first)
    positions = jnp.arange(length, dtype=jnp.int32)
    valid = (positions[None, :] < chain_lengths[:, None]) & (
        (residue_mask == 1) | (positions[None, :] == 0)
    )
    silu_cond = jax.nn.silu(time_cond).astype(jnp.bfloat16)
    modulation = jnp.dot(silu_cond, mod_weight, preferred_element_type=jnp.float32) + mod_bias
    scale_a, shift_a, gate_a, scale_t, shift_t, gate_t = [
        modulation[:, None, section * width : (section + 1) * width] for section in range(6)
    ]
    pair_norm, pair_inv = layer_norm(pair_input.astype(jnp.float32))
    pair_normed = (pair_norm * pair_gain).astype(jnp.bfloat16)
    bias_rows = jnp.einsum(
        "cqkp,ph->chqk", pair_normed, pair_weight, preferred_element_type=jnp.float32
    ).astype(jnp.bfloat16)
    biases = lax.all_to_all(bias_rows, "head", split_axis=1, concat_axis=2, tiled=True)
    residues = x_rows.astype(jnp.float32)
    norm_in, inv_in = layer_norm(residues)
    normed_a = (norm_in * (1.0 + scale_a) + shift_a).astype(jnp.bfloat16)
    projected = jnp.einsum(
        "cld,dtf->tclf", normed_a, qkv_weight, preferred_element_type=jnp.float32
    ).astype(jnp.bfloat16)
    queries = head_split(projected[0])
    keys = head_split(projected[1])
    values = head_split(projected[2])
    scores = attn_scores(queries, keys, biases, valid)
    row_max = jnp.max(scores, axis=-1, keepdims=True)
    exp_scores = jnp.exp(scores - row_max)
    row_total = jnp.sum(exp_scores, axis=-1, keepdims=True)
    attn_probs = exp_scores / row_total
    probs_low = attn_probs.astype(jnp.bfloat16)
    mixed = jnp.einsum("chqk,ckhe->cqhe", probs_low, values, preferred_element_type=jnp.float32)
    mixed = mixed.reshape(mixed.shape[:2] + (-1,)).astype(jnp.bfloat16)
    attn_part = jnp.einsum("clf,fd->cld", mixed, out_weight, preferred_element_type=jnp.float32)
    attn_branch = head_sum(attn_part) + out_bias
    sig_a = jax.nn.sigmoid(gate_a)
    middle = residues + sig_a * attn_branch
    norm_mid, inv_mid = layer_norm(middle)
    normed_t = (norm_mid * (1.0 + scale_t) + shift_t).astype(jnp.bfloat16)
    gate_up = jnp.einsum(
        "cld,dtf->tclf", normed_t, gate_up_weight, preferred_element_type=jnp.float32
    )
    hidden = (jax.nn.silu(gate_up[0]) * gate_up[1]).astype(jnp.bfloat16)
    ffn_part = jnp.einsum(
        "clf,fd->cld", hidden, down_weight, preferred_element_type=jnp.float32
    ).astype(jnp.bfloat16)
    ffn_branch = ffn_part.astype(jnp.float32) + swap_heads(ffn_part).astype(jnp.float32)
    sig_t = jax.nn.sigmoid(gate_t)
    layer_output = own_rows((middle + sig_t * ffn_branch).astype(jnp.bfloat16), head, rows)
    grad_out = g_rows.astype(jnp.float32)
    d_ffn = (grad_out * sig_t).astype(jnp.bfloat16)
    d_gate_t = jnp.sum(grad_out * ffn_branch * sig_t * (1.0 - sig_t), axis=1)
    down_grad_t = jnp.einsum("cld,clf->df", d_ffn, hidden, preferred_element_type=jnp.float32)
    d_hidden = jnp.einsum("cld,fd->clf", d_ffn, down_weight, preferred_element_type=jnp.float32)
    d_gate = d_hidden * gate_up[1] * silu_slope(gate_up[0])
    d_up = d_hidden * jax.nn.silu(gate_up[0])
    d_gate_up = jnp.stack([d_gate, d_up]).astype(jnp.bfloat16)
    gate_up_grad = jnp.einsum(
        "cld,tclf->dtf", normed_t, d_gate_up, preferred_element_type=jnp.float32
    )
    ffn_in_part = jnp.einsum(
        "tclf,dtf->cld", d_gate_up, gate_up_weight, preferred_element_type=jnp.float32
    )
    d_normed_t = head_sum(ffn_in_part)
    d_middle = grad_out + norm_back(norm_mid, inv_mid, d_normed_t * (1.0 + scale_t))
    d_scale_t = jnp.sum(d_normed_t * norm_mid, axis=1)
    d_shift_t = jnp.sum(d_normed_t, axis=1)
    d_attn = d_middle * sig_a
    d_gate_a = jnp.sum(d_middle * attn_branch * sig_a * (1.0 - sig_a), axis=1)
    d_out_bias = jnp.sum(d_attn, axis=(0, 1))
    d_attn_low = d_attn.astype(jnp.bfloat16)
    out_weight_grad_t = jnp.einsum(
        "cld,clf->df", d_attn_low, mixed, preferred_element_type=jnp.float32
    )
    d_mixed = head_split(
        jnp.einsum(
            "cld,fd->clf", d_attn_low, out_weight, preferred_element_type=jnp.float32
        ).astype(jnp.bfloat16)
    )
    d_values = jnp.einsum("chqk,cqhe->ckhe", probs_low, d_mixed, preferred_element_type=jnp.float32)
    d_probs = jnp.einsum("cqhe,ckhe->chqk", d_mixed, values, preferred_element_type=jnp.float32)
    d_scores = (
        attn_probs * (d_probs - jnp.sum(d_probs * attn_probs, axis=-1, keepdims=True))
    ).astype(jnp.bfloat16)
    d_queries = jnp.einsum(
        "chqk,ckhe->cqhe", d_scores, keys, preferred_element_type=jnp.float32
    ) * DH ** (-0.5)
    d_keys = jnp.einsum(
        "chqk,cqhe->ckhe", d_scores, queries, preferred_element_type=jnp.float32
    ) * DH ** (-0.5)
    d_qkv = (
        jnp.stack([d_queries, d_keys, d_values]).reshape(3, chains, length, -1).astype(jnp.bfloat16)
    )
    qkv_grad = jnp.einsum("cld,tclf->dtf", normed_a, d_qkv, preferred_element_type=jnp.float32)
    packed = jnp.concatenate(
        [
            to_chunks(qkv_grad, data_count),
            to_chunks(out_weight_grad_t, data_count),
            to_chunks(gate_up_grad, data_count),
            to_chunks(down_grad_t, data_count),
        ],
        axis=1,
    ).astype(jnp.bfloat16)
    reduced = lax.psum_scatter(packed, "dp", scatter_dimension=0, tiled=True)[0].astype(jnp.float32)
    attn_in_part = jnp.einsum(
        "tclf,dtf->cld", d_qkv, qkv_weight, preferred_element_type=jnp.float32
    ).astype(jnp.bfloat16)
    d_normed_a = attn_in_part.astype(jnp.float32) + swap_heads(attn_in_part).astype(jnp.float32)
    input_grad = own_rows(
        d_middle + norm_back(norm_in, inv_in, d_normed_a * (1.0 + scale_a)), head, rows
    )
    d_scale_a = jnp.sum(d_normed_a * norm_in, axis=1)
    d_shift_a = jnp.sum(d_normed_a, axis=1)
    d_modulation = jnp.concatenate(
        [d_scale_a, d_shift_a, d_gate_a, d_scale_t, d_shift_t, d_gate_t], axis=-1
    )
    d_bias_rows = lax.all_to_all(d_scores, "head", split_axis=2, concat_axis=1, tiled=True)
    pair_weight_grad = jnp.einsum(
        "cqkp,chqk->ph", pair_normed, d_bias_rows, preferred_element_type=jnp.float32
    )
    d_pair_normed = jnp.einsum(
        "chqk,ph->cqkp", d_bias_rows, pair_weight, preferred_element_type=jnp.float32
    )
    pair_gain_grad = jnp.sum(d_pair_normed * pair_norm, axis=(0, 1, 2))
    pair_grad = norm_back(pair_norm, pair_inv, d_pair_normed * pair_gain).astype(jnp.bfloat16)
    pair_small = head_sum(jnp.concatenate([pair_weight_grad.reshape(-1), pair_gain_grad])[None])
    small = jnp.concatenate([d_modulation, time_cond, pair_small, d_out_bias[None]], axis=-1)
    small_rows = lax.all_gather(small, "dp", axis=0, tiled=True)
    mod_size = d_modulation.shape[-1]
    cond_size = time_cond.shape[-1]
    pw_size = pair_weight.size
    pg_size = pair_gain.size
    mod_chain = small_rows[:, :mod_size]
    cond_chain = small_rows[:, mod_size : mod_size + cond_size]
    rest = jnp.sum(small_rows[:, mod_size + cond_size :], axis=0)
    pair_weight_grad = rest[:pw_size].reshape(pair_weight.shape)
    pair_gain_grad = rest[pw_size : pw_size + pg_size]
    out_bias_grad = rest[pw_size + pg_size :]
    cond_act = lax.optimization_barrier(jax.nn.silu(cond_chain).astype(jnp.bfloat16)).astype(
        jnp.float32
    )
    mod_weight_grad = jnp.dot(cond_act.T, mod_chain, precision=precise)
    mod_bias_grad = jnp.sum(mod_chain, axis=0)
    cond_grad = jnp.dot(
        d_modulation, mod_weight.astype(jnp.float32).T, precision=precise
    ) * silu_slope(time_cond)
    sizes = [
        qkv_grad.size // data_count,
        out_weight_grad_t.size // data_count,
        gate_up_grad.size // data_count,
        down_grad_t.size // data_count,
    ]
    flat = reduced.reshape(-1)
    offsets = [0]
    for size in sizes:
        offsets.append(offsets[-1] + size)
    pieces = [flat[offsets[i] : offsets[i + 1]] for i in range(4)]
    qkv_grad = pieces[0].reshape((-1,) + qkv_grad.shape[1:])
    out_weight_grad = pieces[1].reshape(-1, out_weight_grad_t.shape[1]).T
    gate_up_grad = pieces[2].reshape((-1,) + gate_up_grad.shape[1:])
    down_grad = pieces[3].reshape(-1, down_grad_t.shape[1]).T
    return (
        layer_output,
        input_grad,
        pair_grad,
        cond_grad,
        mod_weight_grad,
        mod_bias_grad,
        qkv_grad,
        pair_gain_grad,
        pair_weight_grad,
        out_weight_grad,
        out_bias_grad,
        gate_up_grad,
        down_grad,
    )


def solution(mesh):
    placed = (
        P("dp", "head", None),
        P("dp", "head", None, None),
        P("dp", None),
        P("dp"),
        P("dp", None),
        P(),
        P(),
        P(None, None, "head"),
        P(),
        P(),
        P("head", None),
        P(),
        P(None, None, "head"),
        P("head", None),
        P("dp", "head", None),
    )
    return jax.shard_map(
        shards,
        mesh=mesh,
        in_specs=placed,
        out_specs=(
            P("dp", "head", None),
            P("dp", "head", None),
            P("dp", "head", None, None),
            P("dp", None),
            P(),
            P(),
            P("dp", None, "head"),
            P(),
            P(),
            P("head", "dp"),
            P(),
            P("dp", None, "head"),
            P("head", "dp"),
        ),
        check_vma=False,
    )
```

profile of v0, /device:TPU:0, one launch (start us, length us, event | category | flops | bytes accessed | tf_op | source)
XLA Modules:
  0.0 375.7 jit_solution(14148207465790848436)
XLA Ops:
  7.2 3.0 collective-permute-start
  10.2 22.4 %copy.116 = bf16[1,128,256,256]{2,3,1,0:T(8,128)(2,1)} copy(bf16[1,128,256,256]{3,2,1,0:T(8,128)(2,1)} %param.16) | data formatting | bytes 33554432 | tf_op args[1]
  32.6 6.9 %convert_reduce_fusion = f32[128,256]{1,0:T(8,128)S(1)} fusion(bf16[1,128,256,256]{2,3,1,0:T(8,128)(2,1)} %copy.116), kind=kLoop, calls=%fused_computation.2 | loop fusion | flops 16744448 | bytes 16908288 | tf_op jit(solution)/shard_map/reduce_sum | solution.py:14
  39.5 3.7 copy-done.2
  43.3 4.7 %fusion.13 = f32[128,256]{1,0:T(8,128)S(1)} fusion(bf16[1,128,256,256]{2,3,1,0:T(8,128)(2,1)S(1)} %copy-done.2, f32[128,256]{1,0:T(8,128)S(1)} %broadcast_multiply_fusion.2), kind=kLoop, calls=%fused_computation.15 | loop fusion | flops 33521664 | bytes 17039360 | tf_op jit(solution)/shard_map/reduce_sum | solution.py:15
  48.0 5.2 %fusion.39 = bf16[1,12,128,256]{3,1,2,0:T(8,128)(2,1)S(1)} fusion(bf16[1,128,256,256]{2,3,1,0:T(8,128)(2,1)S(1)} %copy-done.2, f32[256]{0:T(256)S(1)} %copy-done.52, f32[128,256]{1,0:T(8,128)S(1)} %add_rsqrt_fusion, f32[128,256]{1,0:T(8,128)S(1)} %broadcast_multiply_fusion.2, bf16[256,12]{0,1:T(8,128)(2,1)S(1)} %copy-done.61), kind=kOutput, calls=%fused_computation.52 | convolution fusion | flops 243662848 | bytes 17832960 | tf_op jit(solution)/shard_map/cqkp,ph->chqk/dot_general | solution.py:100
  54.4 3.7 all-to-all-start
  73.6 3.7 copy.120
  77.3 3.4 reshape.1017
  85.2 3.1 convolution_convert_fusion.8
  92.5 17.9 %collective-permute-done.1 = f32[1,256,768]{2,1,0:T(8,128)} collective-permute-done((f32[1,256,768]{2,1,0:T(8,128)S(1)}, f32[1,256,768]{2,1,0:T(8,128)}, u32[]{:S(2)}, u32[]{:S(2)}) %collective-permute-start.1) | collective-permute-done | bytes 786464 | tf_op jit(solution)/shard_map/ppermute | solution.py:35
  112.3 4.0 %fusion.19 = f32[2,1,256,1536]{3,2,0,1:T(8,128)S(1)} fusion(bf16[768,2,1536]{2,1,0:T(2,128)(2,1)} %param.27, f32[1,256,768]{2,1,0:T(8,128)S(1)} %get-tuple-element.87, f32[768]{0:T(1024)} %get-tuple-element.78, f32[768]{0:T(1024)S(1)} %get-tuple-element.79, f32[256]{0:T(256)S(1)} %add_rsqrt_fusion.1, f32[256]{0:T(256)S(1)} %broadcast_multiply_fusion.7), kind=kOutput, calls=%fused_computation.25 | convolution fusion | flops 1208942592 | bytes 8658944 | tf_op jit(solution)/shard_map/cld,dtf->tclf/dot_general | solution.py:127
  123.4 3.4 convolution_convert_fusion.1
  126.8 5.8 %reshape.1011 = bf16[16,576,128]{2,1,0:T(8,128)(2,1)} reshape(bf16[768,1536]{1,0:T(8,128)(2,1)} %convolution_convert_fusion.1) | data formatting | bytes 4718592 | tf_op jit(solution)/shard_map/reshape | solution.py:60
  132.6 5.1 %convolution_convert_fusion = bf16[768,2,1536]{2,0,1:T(8,128)(2,1)} fusion(bf16[1,256,1536]{2,1,0:T(8,128)(2,1)} %copy-done.23, bf16[1,256,1536]{2,1,0:T(8,128)(2,1)} %copy-done.22, f32[1,256,768]{2,1,0:T(8,128)S(1)} %get-tuple-element.87, f32[768]{0:T(1024)} %get-tuple-element.78, f32[768]{0:T(1024)S(1)} %get-tuple-element.79, f32[256]{0:T(256)} %copy-done.46, ...), kind=kOutput, calls=%fused_computation.19 | convolution fusion | flops 1214447616 | bytes 7086080 | tf_op jit(solution)/shard_map/cld,tclf->dtf/dot_general | solution.py:145
  137.7 9.3 %copy.141 = bf16[768,2,1536]{2,1,0:T(2,128)(2,1)} copy(bf16[768,2,1536]{2,0,1:T(8,128)(2,1)} %convolution_convert_fusion) | data formatting | bytes 9437184 | tf_op jit(solution)/shard_map/convert.10
  147.0 11.4 %reshape.1010 = bf16[16,1152,128]{2,1,0:T(8,128)(2,1)} reshape(bf16[768,2,1536]{2,1,0:T(2,128)(2,1)} %copy.141) | data formatting | bytes 9437184 | tf_op jit(solution)/shard_map/reshape | solution.py:60
  167.6 3.2 convolution_convert_fusion.6
  185.3 2.9 copy.139
  188.3 5.4 %reshape.1008 = bf16[16,432,128]{2,1,0:T(8,128)(2,1)} reshape(bf16[768,3,384]{2,1,0:T(4,128)(2,1)} %copy.139) | data formatting | bytes 3538944 | tf_op jit(solution)/shard_map/reshape | solution.py:60
  193.6 7.5 %pad_maximum_fusion = bf16[16,2304,128]{2,1,0:T(8,128)(2,1)} fusion(bf16[16,576,128]{2,1,0:T(8,128)(2,1)} %reshape.1011, bf16[16,1152,128]{2,1,0:T(8,128)(2,1)} %reshape.1010, bf16[16,144,128]{2,1,0:T(8,128)(2,1)} %reshape.1009, bf16[16,432,128]{2,1,0:T(8,128)(2,1)} %reshape.1008), kind=kLoop, calls=%fused_computation.18 | loop fusion | flops 37748736 | bytes 18874368 | tf_op jit(solution)/shard_map/concatenate | solution.py:182
  201.2 3.0 fusion.48
  207.7 8.2 %collective-permute-done.2 = bf16[1,256,768]{2,1,0:T(8,128)(2,1)S(1)} collective-permute-done((bf16[1,256,768]{2,1,0:T(8,128)(2,1)S(1)}, bf16[1,256,768]{2,1,0:T(8,128)(2,1)S(1)}, u32[]{:S(2)}, u32[]{:S(2)}) %collective-permute-start.2) | collective-permute-done | bytes 393248 | tf_op jit(solution)/shard_map/ppermute | solution.py:35
  219.8 3.6 all-to-all-start.1
  226.1 6.8 %all-to-all-done.1 = bf16[1,6,256,256]{3,1,0,2:T(8,128)(2,1)S(1)} async-done(((bf16[1,6,256,256]{3,1,0,2:T(8,128)(2,1)}), bf16[1,6,256,256]{3,1,0,2:T(8,128)(2,1)S(1)}, u32[]{:S(2)}, u32[]{:S(2)}) %all-to-all-start.1) | async-done | bytes 786464 | tf_op jit(solution)/shard_map/all_to_all | solution.py:204
  233.1 10.0 %fusion.51 = f32[256,12]{1,0:T(8,128)S(1)} fusion(bf16[1,128,256,256]{2,3,1,0:T(8,128)(2,1)} %copy.116, f32[256]{0:T(256)S(1)} %copy-done.53, f32[128,256]{1,0:T(8,128)S(1)} %copy-done.29, f32[128,256]{1,0:T(8,128)S(1)} %copy-done.21, bf16[12,128,256]{2,1,0:T(8,128)(2,1)S(1)} %bitcast.217), kind=kOutput, calls=%fused_computation.73 | convolution fusion | flops 243269632 | bytes 17839104 | tf_op jit(solution)/shard_map/cqkp,chqk->ph/dot_general | solution.py:205
  243.3 21.5 %fusion.12 = (f32[256]{0:T(256)S(1)}, f32[128,256]{1,0:T(8,128)S(1)}, f32[128,256,256]{1,2,0:T(8,128)}) fusion(bf16[1,128,256,256]{2,3,1,0:T(8,128)(2,1)} %copy.116, f32[128,256]{1,0:T(8,128)S(1)} %copy-done.29, f32[128,256]{1,0:T(8,128)S(1)} %copy-done.21, f32[256]{0:T(256)S(1)} %copy-done.53, bf16[256,12]{0,1:T(8,128)(2,1)S(1)} %copy-done.62, ...), kind=kOutput, calls=%fused_computation.14 | convolution fusion | flops 268402432 | bytes 51519488 | tf_op jit(solution)/shard_map/chqk,ph->cqkp/dot_general | solution.py:208
  265.4 15.1 %multiply_reduce_fusion = f32[128,256]{1,0:T(8,128)S(1)} fusion(f32[128,256,256]{1,2,0:T(8,128)} %get-tuple-element.115, f32[256]{0:T(256)S(1)} %copy-done.53), kind=kLoop, calls=%fused_computation.16 | loop fusion | flops 16744448 | bytes 33686528 | tf_op jit(solution)/shard_map/reduce_sum | solution.py:20
  284.0 24.9 %fusion.11 = bf16[1,128,256,256]{2,3,1,0:T(8,128)(2,1)} fusion(bf16[1,128,256,256]{2,3,1,0:T(8,128)(2,1)} %copy.116, f32[128,256,256]{1,2,0:T(8,128)} %get-tuple-element.115, f32[128,256]{1,0:T(8,128)S(1)} %broadcast_multiply_fusion, f32[128,256]{1,0:T(8,128)S(1)} %broadcast_multiply_fusion.1, f32[256]{0:T(256)S(1)} %copy-done.53, ...), kind=kLoop, calls=%fused_computation.13 | loop fusion | flops 75497472 | bytes 67634176 | tf_op jit(solution)/shard_map/convert_element_type | solution.py:212
  308.9 22.4 %copy.142 = bf16[1,128,256,256]{3,2,1,0:T(8,128)(2,1)} copy(bf16[1,128,256,256]{2,3,1,0:T(8,128)(2,1)} %fusion.11) | data formatting | bytes 33554432
  331.3 23.8 %all-gather = f32[16,1,8960]{2,1,0:T(1,128)S(1)} all-gather(f32[1,1,8960]{2,1,0:T(1,128)S(1)} %bitcast.228), channel_id=1, replica_groups=mesh['dp'=16,'head'=2] {'dp'}, dimensions={0}, use_global_device_ids=true | all-gather | bytes 609280 | tf_op jit(solution)/shard_map/all_gather | solution.py:215
  357.9 4.2 %fusion.77 = f32[256,4608]{1,0:T(8,128)} fusion(bf16[16,256]{1,0:T(8,128)(2,1)S(1)} %multiply_convert_fusion.8, f32[16,8960]{1,0:T(8,128)S(1)} %bitcast.202), kind=kOutput, calls=%fused_computation.129 | convolution fusion | flops 226492416 | bytes 5021696 | tf_op jit(solution)/shard_map/dot_general | solution.py:229
  (237 shorter events, 80.6 us)
Async XLA Ops:
  7.2 109.2 %copy-start = (bf16[1536,768]{1,0:T(8,128)(2,1)S(1)}, bf16[1536,768]{1,0:T(8,128)(2,1)}, u32[]{:S(2)}) copy-start(bf16[1536,768]{1,0:T(8,128)(2,1)} %param.28) | copy-start | bytes 7077892
  7.2 56.3 %collective-permute-start = (bf16[1,128,768]{2,1,0:T(8,128)(2,1)}, bf16[1,128,768]{2,1,0:T(8,128)(2,1)S(1)}, u32[]{:S(2)}, u32[]{:S(2)}) collective-permute-start(bf16[1,128,768]{2,1,0:T(8,128)(2,1)} %param.15), channel_id=1, source_target_pairs={{0,1},{1,0},{2,3},{3,2},{4,5},{5,4},{6,7},{7,6},{8,9},{9,8},{10,11... | collective-permute-start | bytes 589832 | tf_op jit(solution)/shard_map/ppermute | solution.py:35
  32.6 10.7 %copy-start.2 = (bf16[1,128,256,256]{2,3,1,0:T(8,128)(2,1)S(1)}, bf16[1,128,256,256]{2,3,1,0:T(8,128)(2,1)}, u32[]{:S(2)}) copy-start(bf16[1,128,256,256]{2,3,1,0:T(8,128)(2,1)} %copy.116) | copy-start | bytes 50331652
  54.4 7.7 %copy-start.58 = (s32[1,256]{1,0:T(1,128)S(1)}, s32[1,256]{1,0:T(1,128)}, u32[]{:S(2)}) copy-start(s32[1,256]{1,0:T(1,128)} %param.19) | copy-start | bytes 3076
  54.4 9.1 %copy-start.12 = (bf16[1,128,768]{2,1,0:T(8,128)(2,1)S(1)}, bf16[1,128,768]{2,1,0:T(8,128)(2,1)}, u32[]{:S(2)}) copy-start(bf16[1,128,768]{2,1,0:T(8,128)(2,1)} %param.15) | copy-start | bytes 589828
  54.4 17.9 %all-to-all-start = ((bf16[1,12,128,256]{3,2,0,1:T(8,128)(2,1)}), bf16[1,12,128,256]{3,2,0,1:T(8,128)(2,1)S(1)}, u32[]{:S(2)}, u32[]{:S(2)}) async-start(bf16[1,12,128,256]{3,2,0,1:T(8,128)(2,1)} %copy.118), calls=%async_computation | async-start | bytes 1572864 | tf_op jit(solution)/shard_map/all_to_all | solution.py:103
  58.0 304.0 %reduce-scatter.2.cloned.1.call-start = ((), (), s32[]{:S(2)}) async-start(), calls=%async_computation.3 | async-start | bytes 10027008 | tf_op jit(solution)/shard_map/reduce_scatter | solution.py:191
  85.2 25.3 %copy-start.41 = (f32[768]{0:T(1024)S(1)}, f32[768]{0:T(1024)}, u32[]{:S(2)}) copy-start(f32[768]{0:T(1024)} %param.26) | copy-start | bytes 9220
  89.8 20.6 %collective-permute-start.1 = (f32[1,256,768]{2,1,0:T(8,128)S(1)}, f32[1,256,768]{2,1,0:T(8,128)}, u32[]{:S(2)}, u32[]{:S(2)}) collective-permute-start(f32[1,256,768]{2,1,0:T(8,128)S(1)} %convolution_bitcast_fusion), channel_id=1, source_target_pairs={{0,1},{1,0},{2,3},{3,2},{4,5},{5,4},{6,7},{7,6},{8,9},{9,8},{10,11... | collective-permute-start | bytes 2359304 | tf_op jit(solution)/shard_map/ppermute | solution.py:35
  91.9 24.5 %collective-permute-start.3 = (bf16[1,128,768]{2,1,0:T(8,128)(2,1)}, bf16[1,128,768]{2,1,0:T(8,128)(2,1)}, u32[]{:S(2)}, u32[]{:S(2)}) collective-permute-start(bf16[1,128,768]{2,1,0:T(8,128)(2,1)} %param.29), channel_id=1, source_target_pairs={{0,1},{1,0},{2,3},{3,2},{4,5},{5,4},{6,7},{7,6},{8,9},{9,8},{10,11... | collective-permute-start | bytes 589832 | tf_op jit(solution)/shard_map/ppermute | solution.py:35
  121.5 37.0 %collective-permute-start.4 = (f32[1,256,768]{2,1,0:T(8,128)}, f32[1,256,768]{2,1,0:T(8,128)}, u32[]{:S(2)}, u32[]{:S(2)}) collective-permute-start(f32[1,256,768]{2,1,0:T(8,128)} %fusion.42), channel_id=1, source_target_pairs={{0,1},{1,0},{2,3},{3,2},{4,5},{5,4},{6,7},{7,6},{8,9},{9,8},{10,11... | collective-permute-start | bytes 2359304 | tf_op jit(solution)/shard_map/ppermute | solution.py:35
  173.8 9.5 %copy-start.40 = (f32[768]{0:T(1024)S(1)}, f32[768]{0:T(1024)}, u32[]{:S(2)}) copy-start(f32[768]{0:T(1024)} %copy-done.39) | copy-start | bytes 9220
  173.8 9.5 %copy-start.51 = (f32[256]{0:T(256)S(1)}, f32[256]{0:T(256)}, u32[]{:S(2)}) copy-start(f32[256]{0:T(256)} %copy-done.50) | copy-start | bytes 3076
  173.8 9.5 %copy-start.55 = (f32[256]{0:T(256)S(1)}, f32[256]{0:T(256)}, u32[]{:S(2)}) copy-start(f32[256]{0:T(256)} %copy-done.54) | copy-start | bytes 3076
  204.2 11.8 %copy-start.27 = (bf16[1,128,768]{2,1,0:T(8,128)(2,1)S(1)}, bf16[1,128,768]{2,1,0:T(8,128)(2,1)}, u32[]{:S(2)}) copy-start(bf16[1,128,768]{2,1,0:T(8,128)(2,1)} %param.29) | copy-start | bytes 589828
  204.2 11.7 %collective-permute-start.2 = (bf16[1,256,768]{2,1,0:T(8,128)(2,1)S(1)}, bf16[1,256,768]{2,1,0:T(8,128)(2,1)S(1)}, u32[]{:S(2)}, u32[]{:S(2)}) collective-permute-start(bf16[1,256,768]{2,1,0:T(8,128)(2,1)S(1)} %fusion.48), channel_id=1, source_target_pairs={{0,1},{1,0},{2,3},{3,2},{4,5},{5,4},{6,7},{7,6},{8,9},{9,8},{10,11... | collective-permute-start | bytes 1179656 | tf_op jit(solution)/shard_map/ppermute | solution.py:35
  205.7 12.4 %copy-start.4 = (bf16[6,256,256]{1,2,0:T(8,128)(2,1)S(1)}, bf16[6,256,256]{1,2,0:T(8,128)(2,1)}, u32[]{:S(2)}) copy-start(bf16[6,256,256]{1,2,0:T(8,128)(2,1)} %copy-done.3) | copy-start | bytes 2359300
  205.7 17.8 %collective-permute-start.5 = (bf16[1,256,768]{2,1,0:T(8,128)(2,1)S(1)}, bf16[1,256,768]{2,1,0:T(8,128)(2,1)}, u32[]{:S(2)}, u32[]{:S(2)}) collective-permute-start(bf16[1,256,768]{2,1,0:T(8,128)(2,1)S(1)} %fusion.47), channel_id=1, source_target_pairs={{0,1},{1,0},{2,3},{3,2},{4,5},{5,4},{6,7},{7,6},{8,9},{9,8},{10,11... | collective-permute-start | bytes 1179656 | tf_op jit(solution)/shard_map/ppermute | solution.py:35
  219.8 13.0 %all-to-all-start.1 = ((bf16[1,6,256,256]{3,1,0,2:T(8,128)(2,1)}), bf16[1,6,256,256]{3,1,0,2:T(8,128)(2,1)S(1)}, u32[]{:S(2)}, u32[]{:S(2)}) async-start(bf16[1,6,256,256]{3,1,0,2:T(8,128)(2,1)} %copy.131), calls=%async_computation.1 | async-start | bytes 2097152 | tf_op jit(solution)/shard_map/all_to_all | solution.py:204
  225.9 7.2 %copy-start.29 = (f32[128,256]{1,0:T(8,128)S(1)}, f32[128,256]{1,0:T(8,128)}, u32[]{:S(2)}) copy-start(f32[128,256]{1,0:T(8,128)} %copy-done.28) | copy-start | bytes 393220
  225.9 7.2 %copy-start.53 = (f32[256]{0:T(256)S(1)}, f32[256]{0:T(256)}, u32[]{:S(2)}) copy-start(f32[256]{0:T(256)} %param.23) | copy-start | bytes 3076
  233.1 10.1 %copy-start.62 = (bf16[256,12]{0,1:T(8,128)(2,1)S(1)}, bf16[256,12]{0,1:T(8,128)(2,1)}, u32[]{:S(2)}) copy-start(bf16[256,12]{0,1:T(8,128)(2,1)} %param.24) | copy-start | bytes 18436
  243.2 22.0 %copy-start.44 = (f32[768]{0:T(1024)S(1)}, f32[768]{0:T(1024)}, u32[]{:S(2)}) copy-start(f32[768]{0:T(1024)} %get-tuple-element.71) | copy-start | bytes 9220
  243.2 22.0 %copy-start.38 = (f32[768]{0:T(1024)S(1)}, f32[768]{0:T(1024)}, u32[]{:S(2)}) copy-start(f32[768]{0:T(1024)} %get-tuple-element.67) | copy-start | bytes 9220
  243.2 22.0 %copy-start.37 = (f32[768]{0:T(1024)S(1)}, f32[768]{0:T(1024)}, u32[]{:S(2)}) copy-start(f32[768]{0:T(1024)} %get-tuple-element.72) | copy-start | bytes 9220
  264.8 66.5 %collective-permute-start.6 = (f32[1,3328]{1,0:T(1,128)S(1)}, f32[1,3328]{1,0:T(1,128)S(1)}, u32[]{:S(2)}, u32[]{:S(2)}) collective-permute-start(f32[1,3328]{1,0:T(1,128)S(1)} %broadcast_in_dim.17), channel_id=1, source_target_pairs={{0,1},{1,0},{2,3},{3,2},{4,5},{5,4},{6,7},{7,6},{8,9},{9,8},{10,11... | collective-permute-start | bytes 39944 | tf_op jit(solution)/shard_map/ppermute | solution.py:35
  265.3 15.2 %copy-start.6 = (f32[1,256,768]{2,1,0:T(8,128)S(1)}, f32[1,256,768]{2,1,0:T(8,128)}, u32[]{:S(2)}) copy-start(f32[1,256,768]{2,1,0:T(8,128)} %copy-done.5) | copy-start | bytes 2359300
  265.3 15.2 %copy-start.15 = (f32[1,256,768]{2,1,0:T(8,128)S(1)}, f32[1,256,768]{2,1,0:T(8,128)}, u32[]{:S(2)}) copy-start(f32[1,256,768]{2,1,0:T(8,128)} %get-tuple-element.98) | copy-start | bytes 2359300
  265.4 15.2 %copy-start.59 = (f32[128]{0:T(128)S(1)}, f32[128]{0:T(128)}, u32[]{:S(2)}) copy-start(f32[128]{0:T(128)} %dynamic-slice.2) | copy-start | bytes 1540
  265.4 16.1 %copy-start.7 = (bf16[256,4608]{1,0:T(8,128)(2,1)S(1)}, bf16[256,4608]{1,0:T(8,128)(2,1)}, u32[]{:S(2)}) copy-start(bf16[256,4608]{1,0:T(8,128)(2,1)} %param.20) | copy-start | bytes 7077892
  265.4 16.1 %copy-start.49 = (f32[1,256]{1,0:T(1,128)S(1)}, f32[1,256]{1,0:T(1,128)}, u32[]{:S(2)}) copy-start(f32[1,256]{1,0:T(1,128)} %param.17) | copy-start | bytes 3076
  308.9 22.4 %copy-start.43 = (f32[768]{0:T(1024)S(1)}, f32[768]{0:T(1024)}, u32[]{:S(2)}) copy-start(f32[768]{0:T(1024)} %get-tuple-element.70) | copy-start | bytes 9220
  (44 other events, 153.3 us)
Sparse Core Ops, SparseCore 0:
  201.3 111.5 reduce-scatter.1
where the time goes:
time: 382 us; the launch traced here: 376 us
  local copies, waits for them, and re-layouts  121 us (32%)
  matrix products  87 us (23%)
  other arithmetic  77.7 us (20%)
  waiting for transfers between devices  33 us (9%)
  blocking collectives  23.8 us (6%)
  starting transfers between devices  17.6 us (5%)
  between operations  16.1 us (4%)
    unnamed x144, local copies, waits for them, and re-layouts  52.1 us
    ppermute x7, waiting for transfers between devices, swap_heads(): return lax.ppermute(values, 'head', [(0, 1), (1, 0)])  26.1 us
    convert_element_type x1, other arithmetic, shards(): norm_back(pair_norm, pair_inv, d_pair_normed * pair_gain)  24.9 us
    reshape x4, local copies, waits for them, and re-layouts, to_chunks(): return values.reshape(parts, -1, LANES)  24.8 us
    all_gather x1, blocking collectives, shards(): small_rows = lax.all_gather(small, 'dp', axis=0, tiled=True)  23.8 us
    dot_general x1, matrix products, shards(): jnp.einsum('chqk,ph->cqkp', d_bias_rows, pair_weight, preferred_element_t...  21.5 us
    reduce_sum x1, other arithmetic, norm_back(): mean_grad = jnp.mean(grad, axis=-1, keepdims=True)  15.1 us
    another operation x2, local copies, waits for them, and re-layouts  12.2 us
  transfers between devices with their start and end apart: 10, of which 3 were waited for; matrix products, arithmetic and copies ran while one was open for 56% of the time, Pallas kernels for 0%

commit v1 on v0

--- a/solution.py
+++ b/solution.py
@@ -201,7 +201,15 @@
     d_modulation = jnp.concatenate(
         [d_scale_a, d_shift_a, d_gate_a, d_scale_t, d_shift_t, d_gate_t], axis=-1
     )
-    d_bias_rows = lax.all_to_all(d_scores, "head", split_axis=2, concat_axis=1, tiled=True)
+    d_bias_rows = jnp.concatenate(
+        lax.all_to_all(
+            jnp.stack(jnp.split(d_scores, lax.axis_size("head"), axis=2)),
+            axis_name="head",
+            split_axis=0,
+            concat_axis=0,
+        ),
+        axis=1,
+    )
     pair_weight_grad = jnp.einsum(
         "cqkp,chqk->ph", pair_normed, d_bias_rows, preferred_element_type=jnp.float32
     )

time: 382 us -> 357 us (0.935)
  waiting for transfers between devices: 33 us -> 24.2 us
  matrix products: 87 us -> 79.5 us
  local copies, waits for them, and re-layouts: 121 us -> 114 us
    ppermute x7, waiting for transfers between devices: 26.1 us -> 17.8 us  [swap_heads(): return lax.ppermute(values, 'head', [(0, 1), (1, 0)])]
    another operation x2 -> x4, local copies, waits for them, and re-layouts: 12.2 us -> 14.3 us
    unnamed x144 -> x138, local copies, waits for them, and re-layouts: 52.1 us -> 52.7 us
  transfers between devices with their start and end apart: 10 -> 10, of which waited for: 3 -> 2; matrix products, arithmetic and copies ran while one was open for 56% -> 69% of each run, Pallas kernels for 0% -> 0%
where the time goes in v1:
time: 357 us; the launch traced here: 351 us
  local copies, waits for them, and re-layouts  114 us (32%)
  matrix products  79.5 us (22%)
  other arithmetic  75.9 us (21%)
  waiting for transfers between devices  24.2 us (7%)
  blocking collectives  23.3 us (7%)
  starting transfers between devices  17.6 us (5%)
  between operations  16.1 us (5%)
    unnamed x138, local copies, waits for them, and re-layouts  52.7 us
    convert_element_type x1, other arithmetic, shards(): norm_back(pair_norm, pair_inv, d_pair_normed * pair_gain)  25.2 us
    all_gather x1, blocking collectives, shards(): small_rows = lax.all_gather(small, 'dp', axis=0, tiled=True)  23.3 us
    reshape x4, local copies, waits for them, and re-layouts, to_chunks(): return values.reshape(parts, -1, LANES)  22 us
    dot_general x1, matrix products, shards(): jnp.einsum('chqk,ph->cqkp', d_bias_rows, pair_weight, preferred_element_t...  21.7 us
    ppermute x7, waiting for transfers between devices, swap_heads(): return lax.ppermute(values, 'head', [(0, 1), (1, 0)])  17.8 us
    reduce_sum x1, other arithmetic, norm_back(): mean_grad = jnp.mean(grad, axis=-1, keepdims=True)  14.8 us
    another operation x3, local copies, waits for them, and re-layouts  14.1 us
  transfers between devices with their start and end apart: 10, of which 2 were waited for; matrix products, arithmetic and copies ran while one was open for 69% of the time, Pallas kernels for 0%

profile of v1, /device:TPU:0, one launch (start us, length us, event | category | flops | bytes accessed | tf_op | source)
XLA Modules:
  0.0 351.0 jit_solution(2505753306162809974)
XLA Ops:
  7.2 3.0 collective-permute-start
  10.2 22.4 %copy.85 = bf16[1,128,256,256]{2,3,1,0:T(8,128)(2,1)} copy(bf16[1,128,256,256]{3,2,1,0:T(8,128)(2,1)} %param.16) | data formatting | bytes 33554432 | tf_op args[1]
  32.6 6.9 %convert_reduce_fusion = f32[128,256]{1,0:T(8,128)S(1)} fusion(bf16[1,128,256,256]{2,3,1,0:T(8,128)(2,1)} %copy.85), kind=kLoop, calls=%fused_computation.2 | loop fusion | flops 16744448 | bytes 16908288 | tf_op jit(solution)/shard_map/reduce_sum | solution.py:14
  39.5 3.7 %copy-done.2 = bf16[1,128,256,256]{2,3,1,0:T(8,128)(2,1)S(1)} copy-done((bf16[1,128,256,256]{2,3,1,0:T(8,128)(2,1)S(1)}, bf16[1,128,256,256]{2,3,1,0:T(8,128)(2,1)}, u32[]{:S(2)}) %copy-start.2) | copy-done | bytes 16777240
  43.3 4.7 %fusion.13 = f32[128,256]{1,0:T(8,128)S(1)} fusion(bf16[1,128,256,256]{2,3,1,0:T(8,128)(2,1)S(1)} %copy-done.2, f32[128,256]{1,0:T(8,128)S(1)} %broadcast_multiply_fusion.2), kind=kLoop, calls=%fused_computation.15 | loop fusion | flops 33521664 | bytes 17039360 | tf_op jit(solution)/shard_map/reduce_sum | solution.py:15
  48.0 5.2 %fusion.39 = bf16[1,12,128,256]{3,1,2,0:T(8,128)(2,1)S(1)} fusion(bf16[1,128,256,256]{2,3,1,0:T(8,128)(2,1)S(1)} %copy-done.2, f32[256]{0:T(256)S(1)} %copy-done.51, f32[128,256]{1,0:T(8,128)S(1)} %add_rsqrt_fusion, f32[128,256]{1,0:T(8,128)S(1)} %broadcast_multiply_fusion.2, bf16[256,12]{0,1:T(8,128)(2,1)S(1)} %copy-done.59), kind=kOutput, calls=%fused_computation.52 | convolution fusion | flops 243662848 | bytes 17832960 | tf_op jit(solution)/shard_map/cqkp,ph->chqk/dot_general | solution.py:100
  54.4 3.7 %all-to-all-start = ((bf16[1,12,128,256]{3,2,0,1:T(8,128)(2,1)}), bf16[1,12,128,256]{3,2,0,1:T(8,128)(2,1)S(1)}, u32[]{:S(2)}, u32[]{:S(2)}) async-start(bf16[1,12,128,256]{3,2,0,1:T(8,128)(2,1)} %copy.87), calls=%async_computation | async-start | bytes 1572864 | tf_op jit(solution)/shard_map/all_to_all | solution.py:103
  73.6 3.7 %copy.89 = f32[1,6,2,128,256]{3,2,4,1,0:T(2,128)} copy(f32[1,6,2,128,256]{4,3,1,2,0:T(8,128)} %convert_bitcast_fusion) | data formatting | bytes 3145728 | tf_op jit(solution)/shard_map/convert_element_type | solution.py:55
  77.3 3.4 reshape.1018
  85.7 2.5 convolution_convert_fusion.8
  91.4 17.8 %collective-permute-done.1 = f32[1,256,768]{2,1,0:T(8,128)S(1)} collective-permute-done((f32[1,256,768]{2,1,0:T(8,128)S(1)}, f32[1,256,768]{2,1,0:T(8,128)S(1)}, u32[]{:S(2)}, u32[]{:S(2)}) %collective-permute-start.1) | collective-permute-done | bytes 786464 | tf_op jit(solution)/shard_map/ppermute | solution.py:35
  110.3 3.8 %fusion.19 = f32[2,1,256,1536]{3,2,0,1:T(8,128)S(1)} fusion(bf16[768,2,1536]{2,1,0:T(2,128)(2,1)} %param.27, f32[1,256,768]{2,1,0:T(8,128)S(1)} %get-tuple-element.74, f32[768]{0:T(1024)S(1)} %copy-done.38, f32[768]{0:T(1024)S(1)} %get-tuple-element.66, f32[256]{0:T(256)S(1)} %add_rsqrt_fusion.1, f32[256]{0:T(256)S(1)} %broadcast_multiply_fusion.7), kind=kOutput, calls=%fused_computation.25 | convolution fusion | flops 1208942592 | bytes 8658944 | tf_op jit(solution)/shard_map/cld,dtf->tclf/dot_general | solution.py:127
  122.5 3.9 %reshape.1012 = bf16[16,576,128]{2,1,0:T(8,128)(2,1)} reshape(bf16[768,1536]{1,0:T(8,128)(2,1)S(1)} %convolution_convert_fusion.1) | data formatting | bytes 4718592 | tf_op jit(solution)/shard_map/reshape | solution.py:60
  126.4 5.1 %convolution_convert_fusion = bf16[768,2,1536]{2,0,1:T(8,128)(2,1)} fusion(bf16[1,256,1536]{2,1,0:T(8,128)(2,1)} %copy-done.21, bf16[1,256,1536]{2,1,0:T(8,128)(2,1)} %copy-done.20, f32[1,256,768]{2,1,0:T(8,128)S(1)} %get-tuple-element.74, f32[768]{0:T(1024)} %get-tuple-element.65, f32[768]{0:T(1024)S(1)} %get-tuple-element.66, f32[256]{0:T(256)} %copy-done.44, ...), kind=kOutput, calls=%fused_computation.19 | convolution fusion | flops 1214447616 | bytes 7086080 | tf_op jit(solution)/shard_map/cld,tclf->dtf/dot_general | solution.py:145
  131.6 9.3 %copy.107 = bf16[768,2,1536]{2,1,0:T(2,128)(2,1)} copy(bf16[768,2,1536]{2,0,1:T(8,128)(2,1)} %convolution_convert_fusion) | data formatting | bytes 9437184 | tf_op jit(solution)/shard_map/convert.10
  140.9 11.4 %reshape.1011 = bf16[16,1152,128]{2,1,0:T(8,128)(2,1)} reshape(bf16[768,2,1536]{2,1,0:T(2,128)(2,1)} %copy.107) | data formatting | bytes 9437184 | tf_op jit(solution)/shard_map/reshape | solution.py:60
  152.3 2.5 multiply_reduce_fusion.2
  158.0 2.5 convolution_convert_fusion.6
  170.8 2.9 copy.105
  173.7 5.4 %reshape.1009 = bf16[16,432,128]{2,1,0:T(8,128)(2,1)} reshape(bf16[768,3,384]{2,1,0:T(4,128)(2,1)} %copy.105) | data formatting | bytes 3538944 | tf_op jit(solution)/shard_map/reshape | solution.py:60
  179.0 7.3 %pad_maximum_fusion = bf16[16,2304,128]{2,1,0:T(8,128)(2,1)} fusion(bf16[16,576,128]{2,1,0:T(8,128)(2,1)} %reshape.1012, bf16[16,1152,128]{2,1,0:T(8,128)(2,1)} %reshape.1011, bf16[16,144,128]{2,1,0:T(8,128)(2,1)S(1)} %reshape.1010, bf16[16,432,128]{2,1,0:T(8,128)(2,1)} %reshape.1009), kind=kLoop, calls=%fused_computation.18 | loop fusion | flops 37748736 | bytes 18874368 | tf_op jit(solution)/shard_map/concatenate | solution.py:182
  189.9 3.5 %all-to-all-start.1 = ((bf16[2,1,6,128,256]{3,4,2,1,0:T(8,128)(2,1)}), bf16[2,1,6,128,256]{3,4,2,1,0:T(8,128)(2,1)S(1)}, u32[]{:S(2)}, u32[]{:S(2)}) async-start(bf16[2,1,6,128,256]{3,4,2,1,0:T(8,128)(2,1)} %pad_maximum_fusion.4), calls=%async_computation.1 | async-start | bytes 1572864 | tf_op jit(solution)/shard_map/all_to_all | solution.py:205
  194.2 2.8 fusion.47
  199.1 6.4 %all-to-all-done.1 = bf16[2,1,6,128,256]{3,4,2,1,0:T(8,128)(2,1)S(1)} async-done(((bf16[2,1,6,128,256]{3,4,2,1,0:T(8,128)(2,1)}), bf16[2,1,6,128,256]{3,4,2,1,0:T(8,128)(2,1)S(1)}, u32[]{:S(2)}, u32[]{:S(2)}) %all-to-all-start.1) | async-done | bytes 786464 | tf_op jit(solution)/shard_map/all_to_all | solution.py:205
  207.4 9.7 %fusion.51 = f32[256,12]{1,0:T(8,128)S(1)} fusion(bf16[12,128,256]{2,0,1:T(8,128)(2,1)} %copy.100, bf16[1,128,256,256]{2,3,1,0:T(8,128)(2,1)} %copy.85, f32[256]{0:T(256)S(1)} %copy-done.52, f32[128,256]{1,0:T(8,128)S(1)} %copy-done.29, f32[128,256]{1,0:T(8,128)S(1)} %copy-done.19), kind=kOutput, calls=%fused_computation.73 | convolution fusion | flops 243269632 | bytes 17839104 | tf_op jit(solution)/shard_map/cqkp,chqk->ph/dot_general | solution.py:213
  218.9 21.7 %fusion.12 = (f32[256]{0:T(256)S(1)}, f32[128,256]{1,0:T(8,128)S(1)}, f32[128,256,256]{1,2,0:T(8,128)}) fusion(bf16[1,128,256,256]{2,3,1,0:T(8,128)(2,1)} %copy.85, f32[128,256]{1,0:T(8,128)S(1)} %copy-done.29, f32[128,256]{1,0:T(8,128)S(1)} %copy-done.19, f32[256]{0:T(256)S(1)} %copy-done.53, bf16[12,128,256]{2,0,1:T(8,128)(2,1)} %copy.100, ...), kind=kOutput, calls=%fused_computation.14 | convolution fusion | flops 268402432 | bytes 51519488 | tf_op jit(solution)/shard_map/chqk,ph->cqkp/dot_general | solution.py:216
  241.2 14.8 %multiply_reduce_fusion = f32[128,256]{1,0:T(8,128)S(1)} fusion(f32[128,256,256]{1,2,0:T(8,128)} %get-tuple-element.104, f32[256]{0:T(256)S(1)} %copy-done.53), kind=kLoop, calls=%fused_computation.16 | loop fusion | flops 16744448 | bytes 33686528 | tf_op jit(solution)/shard_map/reduce_sum | solution.py:20
  257.0 2.5 convolution_multiply_fusion.2
  259.5 25.2 %fusion.11 = bf16[1,128,256,256]{2,3,1,0:T(8,128)(2,1)} fusion(bf16[1,128,256,256]{2,3,1,0:T(8,128)(2,1)} %copy.85, f32[128,256,256]{1,2,0:T(8,128)} %get-tuple-element.104, f32[128,256]{1,0:T(8,128)S(1)} %broadcast_multiply_fusion, f32[128,256]{1,0:T(8,128)S(1)} %broadcast_multiply_fusion.1, f32[256]{0:T(256)S(1)} %copy-done.53, ...), kind=kLoop, calls=%fused_computation.13 | loop fusion | flops 75497472 | bytes 67634176 | tf_op jit(solution)/shard_map/convert_element_type | solution.py:220
  284.7 22.4 %copy.108 = bf16[1,128,256,256]{3,2,1,0:T(8,128)(2,1)} copy(bf16[1,128,256,256]{2,3,1,0:T(8,128)(2,1)} %fusion.11) | data formatting | bytes 33554432
  307.2 23.3 %all-gather = f32[16,1,8960]{2,1,0:T(1,128)S(1)} all-gather(f32[1,1,8960]{2,1,0:T(1,128)S(1)} %bitcast.231), channel_id=1, replica_groups=mesh['dp'=16,'head'=2] {'dp'}, dimensions={0}, use_global_device_ids=true | all-gather | bytes 609280 | tf_op jit(solution)/shard_map/all_gather | solution.py:223
  333.2 4.2 %fusion.74 = f32[256,4608]{1,0:T(8,128)} fusion(bf16[16,256]{1,0:T(8,128)(2,1)S(1)} %multiply_convert_fusion.8, f32[16,8960]{1,0:T(8,128)S(1)} %bitcast.205), kind=kOutput, calls=%fused_computation.129 | convolution fusion | flops 226492416 | bytes 5021696 | tf_op jit(solution)/shard_map/dot_general | solution.py:237
  (231 shorter events, 67.3 us)
Async XLA Ops:
  7.2 107.0 %copy-start = (bf16[1536,768]{1,0:T(8,128)(2,1)S(1)}, bf16[1536,768]{1,0:T(8,128)(2,1)}, u32[]{:S(2)}) copy-start(bf16[1536,768]{1,0:T(8,128)(2,1)} %param.28) | copy-start | bytes 7077892
  7.2 56.3 %collective-permute-start = (bf16[1,128,768]{2,1,0:T(8,128)(2,1)}, bf16[1,128,768]{2,1,0:T(8,128)(2,1)S(1)}, u32[]{:S(2)}, u32[]{:S(2)}) collective-permute-start(bf16[1,128,768]{2,1,0:T(8,128)(2,1)} %param.15), channel_id=1, source_target_pairs={{0,1},{1,0},{2,3},{3,2},{4,5},{5,4},{6,7},{7,6},{8,9},{9,8},{10,11... | collective-permute-start | bytes 589832 | tf_op jit(solution)/shard_map/ppermute | solution.py:35
  32.6 10.7 %copy-start.2 = (bf16[1,128,256,256]{2,3,1,0:T(8,128)(2,1)S(1)}, bf16[1,128,256,256]{2,3,1,0:T(8,128)(2,1)}, u32[]{:S(2)}) copy-start(bf16[1,128,256,256]{2,3,1,0:T(8,128)(2,1)} %copy.85) | copy-start | bytes 50331652
  53.2 6.1 %copy-start.47 = (f32[1,256]{1,0:T(1,128)S(1)}, f32[1,256]{1,0:T(1,128)}, u32[]{:S(2)}) copy-start(f32[1,256]{1,0:T(1,128)} %param.17) | copy-start | bytes 3076
  54.4 7.7 %copy-start.57 = (s32[1,256]{1,0:T(1,128)S(1)}, s32[1,256]{1,0:T(1,128)}, u32[]{:S(2)}) copy-start(s32[1,256]{1,0:T(1,128)} %param.19) | copy-start | bytes 3076
  54.4 9.1 %copy-start.8 = (bf16[1,128,768]{2,1,0:T(8,128)(2,1)S(1)}, bf16[1,128,768]{2,1,0:T(8,128)(2,1)}, u32[]{:S(2)}) copy-start(bf16[1,128,768]{2,1,0:T(8,128)(2,1)} %param.15) | copy-start | bytes 589828
  54.4 17.9 %all-to-all-start = ((bf16[1,12,128,256]{3,2,0,1:T(8,128)(2,1)}), bf16[1,12,128,256]{3,2,0,1:T(8,128)(2,1)S(1)}, u32[]{:S(2)}, u32[]{:S(2)}) async-start(bf16[1,12,128,256]{3,2,0,1:T(8,128)(2,1)} %copy.87), calls=%async_computation | async-start | bytes 1572864 | tf_op jit(solution)/shard_map/all_to_all | solution.py:103
  58.0 279.4 %reduce-scatter.2.cloned.1.call-start = ((), (), s32[]{:S(2)}) async-start(), calls=%async_computation.3 | async-start | bytes 10027008 | tf_op jit(solution)/shard_map/reduce_scatter | solution.py:191
  85.7 23.4 %copy-start.39 = (f32[768]{0:T(1024)S(1)}, f32[768]{0:T(1024)}, u32[]{:S(2)}) copy-start(f32[768]{0:T(1024)} %param.26) | copy-start | bytes 9220
  88.3 22.1 %copy-start.38 = (f32[768]{0:T(1024)S(1)}, f32[768]{0:T(1024)}, u32[]{:S(2)}) copy-start(f32[768]{0:T(1024)} %get-tuple-element.65) | copy-start | bytes 9220
  88.7 20.5 %copy-start.4 = (f32[1,256,768]{2,1,0:T(8,128)}, f32[1,256,768]{2,1,0:T(8,128)S(1)}, u32[]{:S(2)}) copy-start(f32[1,256,768]{2,1,0:T(8,128)S(1)} %convolution_bitcast_fusion) | copy-start | bytes 2359300
  88.7 20.5 %collective-permute-start.1 = (f32[1,256,768]{2,1,0:T(8,128)S(1)}, f32[1,256,768]{2,1,0:T(8,128)S(1)}, u32[]{:S(2)}, u32[]{:S(2)}) collective-permute-start(f32[1,256,768]{2,1,0:T(8,128)S(1)} %convolution_bitcast_fusion), channel_id=1, source_target_pairs={{0,1},{1,0},{2,3},{3,2},{4,5},{5,4},{6,7},{7,6},{8,9},{9,8},{10,11... | collective-permute-start | bytes 2359304 | tf_op jit(solution)/shard_map/ppermute | solution.py:35
  90.7 27.2 %collective-permute-start.3 = (bf16[1,128,768]{2,1,0:T(8,128)(2,1)}, bf16[1,128,768]{2,1,0:T(8,128)(2,1)S(1)}, u32[]{:S(2)}, u32[]{:S(2)}) collective-permute-start(bf16[1,128,768]{2,1,0:T(8,128)(2,1)} %param.29), channel_id=1, source_target_pairs={{0,1},{1,0},{2,3},{3,2},{4,5},{5,4},{6,7},{7,6},{8,9},{9,8},{10,11... | collective-permute-start | bytes 589832 | tf_op jit(solution)/shard_map/ppermute | solution.py:35
  115.9 71.1 %collective-permute-start.2 = (bf16[1,256,768]{2,1,0:T(8,128)(2,1)}, bf16[1,256,768]{2,1,0:T(8,128)(2,1)}, u32[]{:S(2)}, u32[]{:S(2)}) collective-permute-start(bf16[1,256,768]{2,1,0:T(8,128)(2,1)} %fusion.48), channel_id=1, source_target_pairs={{0,1},{1,0},{2,3},{3,2},{4,5},{5,4},{6,7},{7,6},{8,9},{9,8},{10,11... | collective-permute-start | bytes 1179656 | tf_op jit(solution)/shard_map/ppermute | solution.py:35
  121.4 30.9 %collective-permute-start.4 = (f32[1,256,768]{2,1,0:T(8,128)}, f32[1,256,768]{2,1,0:T(8,128)}, u32[]{:S(2)}, u32[]{:S(2)}) collective-permute-start(f32[1,256,768]{2,1,0:T(8,128)} %fusion.42), channel_id=1, source_target_pairs={{0,1},{1,0},{2,3},{3,2},{4,5},{5,4},{6,7},{7,6},{8,9},{9,8},{10,11... | collective-permute-start | bytes 2359304 | tf_op jit(solution)/shard_map/ppermute | solution.py:35
  140.9 11.5 %copy-start.45 = (f32[256]{0:T(256)S(1)}, f32[256]{0:T(256)}, u32[]{:S(2)}) copy-start(f32[256]{0:T(256)} %copy-done.44) | copy-start | bytes 3076
  163.3 5.4 %copy-start.50 = (f32[256]{0:T(256)S(1)}, f32[256]{0:T(256)}, u32[]{:S(2)}) copy-start(f32[256]{0:T(256)} %copy-done.49) | copy-start | bytes 3076
  163.3 5.4 %copy-start.55 = (f32[256]{0:T(256)S(1)}, f32[256]{0:T(256)}, u32[]{:S(2)}) copy-start(f32[256]{0:T(256)} %copy-done.54) | copy-start | bytes 3076
  189.9 15.6 %all-to-all-start.1 = ((bf16[2,1,6,128,256]{3,4,2,1,0:T(8,128)(2,1)}), bf16[2,1,6,128,256]{3,4,2,1,0:T(8,128)(2,1)S(1)}, u32[]{:S(2)}, u32[]{:S(2)}) async-start(bf16[2,1,6,128,256]{3,4,2,1,0:T(8,128)(2,1)} %pad_maximum_fusion.4), calls=%async_computation.1 | async-start | bytes 1572864 | tf_op jit(solution)/shard_map/all_to_all | solution.py:205
  194.2 13.2 %copy-start.19 = (f32[128,256]{1,0:T(8,128)S(1)}, f32[128,256]{1,0:T(8,128)}, u32[]{:S(2)}) copy-start(f32[128,256]{1,0:T(8,128)} %copy-done.18) | copy-start | bytes 393220
  194.2 13.2 %copy-start.29 = (f32[128,256]{1,0:T(8,128)S(1)}, f32[128,256]{1,0:T(8,128)}, u32[]{:S(2)}) copy-start(f32[128,256]{1,0:T(8,128)} %copy-done.28) | copy-start | bytes 393220
  194.2 13.2 %copy-start.52 = (f32[256]{0:T(256)S(1)}, f32[256]{0:T(256)}, u32[]{:S(2)}) copy-start(f32[256]{0:T(256)} %param.23) | copy-start | bytes 3076
  197.0 20.2 %collective-permute-start.5 = (bf16[1,256,768]{2,1,0:T(8,128)(2,1)S(1)}, bf16[1,256,768]{2,1,0:T(8,128)(2,1)}, u32[]{:S(2)}, u32[]{:S(2)}) collective-permute-start(bf16[1,256,768]{2,1,0:T(8,128)(2,1)S(1)} %fusion.47), channel_id=1, source_target_pairs={{0,1},{1,0},{2,3},{3,2},{4,5},{5,4},{6,7},{7,6},{8,9},{9,8},{10,11... | collective-permute-start | bytes 1179656 | tf_op jit(solution)/shard_map/ppermute | solution.py:35
  218.9 22.2 %copy-start.42 = (f32[768]{0:T(1024)S(1)}, f32[768]{0:T(1024)}, u32[]{:S(2)}) copy-start(f32[768]{0:T(1024)} %get-tuple-element.58) | copy-start | bytes 9220
  218.9 22.2 %copy-start.35 = (f32[768]{0:T(1024)S(1)}, f32[768]{0:T(1024)}, u32[]{:S(2)}) copy-start(f32[768]{0:T(1024)} %get-tuple-element.54) | copy-start | bytes 9220
  218.9 22.2 %copy-start.34 = (f32[768]{0:T(1024)S(1)}, f32[768]{0:T(1024)}, u32[]{:S(2)}) copy-start(f32[768]{0:T(1024)} %get-tuple-element.59) | copy-start | bytes 9220
  240.6 66.5 %collective-permute-start.6 = (f32[1,3328]{1,0:T(1,128)S(1)}, f32[1,3328]{1,0:T(1,128)S(1)}, u32[]{:S(2)}, u32[]{:S(2)}) collective-permute-start(f32[1,3328]{1,0:T(1,128)S(1)} %broadcast_in_dim.17), channel_id=1, source_target_pairs={{0,1},{1,0},{2,3},{3,2},{4,5},{5,4},{6,7},{7,6},{8,9},{9,8},{10,11... | collective-permute-start | bytes 39944 | tf_op jit(solution)/shard_map/ppermute | solution.py:35
  241.2 14.9 %copy-start.58 = (f32[128]{0:T(128)S(1)}, f32[128]{0:T(128)}, u32[]{:S(2)}) copy-start(f32[128]{0:T(128)} %dynamic-slice.2) | copy-start | bytes 1540
  241.2 15.8 %copy-start.3 = (bf16[256,4608]{1,0:T(8,128)(2,1)S(1)}, bf16[256,4608]{1,0:T(8,128)(2,1)}, u32[]{:S(2)}) copy-start(bf16[256,4608]{1,0:T(8,128)(2,1)} %param.20) | copy-start | bytes 7077892
  241.2 15.8 %copy-start.48 = (f32[1,256]{1,0:T(1,128)S(1)}, f32[1,256]{1,0:T(1,128)}, u32[]{:S(2)}) copy-start(f32[1,256]{1,0:T(1,128)} %param.17) | copy-start | bytes 3076
  284.7 22.5 %copy-start.41 = (f32[768]{0:T(1024)S(1)}, f32[768]{0:T(1024)}, u32[]{:S(2)}) copy-start(f32[768]{0:T(1024)} %get-tuple-element.57) | copy-start | bytes 9220
  337.4 5.5 %copy-start.13 = (bf16[1,2304,128]{2,1,0:T(8,128)(2,1)S(1)}, bf16[1,2304,128]{2,1,0:T(8,128)(2,1)}, u32[]{:S(2)}) copy-start(bf16[1,2304,128]{2,1,0:T(8,128)(2,1)} %reduce-scatter.2.cloned.1.call-done) | copy-start | bytes 1769476
  (41 other events, 115.3 us)
Sparse Core Ops, SparseCore 0:
  186.5 112.8 reduce-scatter.1
